TPU v7x, 512 devices: a whole 4x8x8 slice. The times are simulated.
512 devices in a mesh: req: 128 (over y, z, core), tp: 4 (over x).
Axes of the slice: x: 4, y: 8, z: 8, core: 2. Of those that a mesh axis runs over, the one named last changes fastest.
Arguments:
- qkv_rows: bfloat16 [32768, 3, 1536], P('req', None, 'tp'), may hold values from -13 to 13
- row_request: int32 [32768], P('req'), may hold values from 0 to 127, as said below
- request_owner: int32 [128], replicated, may hold values from 0 to 127, each once
- cached_len: int32 [128], P('req'), may hold values from 0 to 1024
- page_table: int32 [128, 8], P('req'), may hold values from 0 to 7, as said below
- kv_pages: bfloat16 [1024, 2, 128, 1536], P('req', None, None, 'tp'), may hold values from -6 to 6
- residual: bfloat16 [32768, 3072], P('req', 'tp'), may hold values from -128 to 128
- out_weight: bfloat16 [1536, 3072], P('tp'), may hold values from -0.15625 to 0.15625
- norm_gain: bfloat16 [3072], P('tp'), may hold values from 0.5 to 1.5
Outputs:
- new_residual: bfloat16 [32768, 3072], P('req', 'tp')
- normed: bfloat16 [32768, 3072], P('req', 'tp')
Inputs may be any that keep to these rules, and one draw needn't show every extreme that they name: `row_request`: on every device at most 5 new tokens name the same request, and one request is named by exactly 5 tokens on every device. Half of the requests are named by exactly one token in all, and no two of those tokens lie on one device. `request_owner`: each device holds the cache of exactly one request. `page_table`: each row names every page of its device's pool once.
All inputs are finite; a program needn't handle non-finite values.
Results may differ from a plain program's by a relative error of at most 0.0093.
The roundings to bfloat16 on the way count: a program that leaves them out, or rounds other values in their place, can miss the bound.
Values may be sent and summed in bfloat16 or wider, within the bound.
No kernel may reach another device: no remote copies, remote signals or barrier semaphores. Data moves between devices by JAX's collectives and lax.ppermute only.
A program may use at most 64 MiB of HBM per device.

v0:
```python
import math
import jax
import jax.numpy as jnp
from jax import lax
from jax.sharding import PartitionSpec as P

D = 3072
HEAD_SIZE = 96
ROPE_BASE = 10000.0
EPS = 1e-05


def rope_tables(position):
    halves = HEAD_SIZE // 2
    inverse = ROPE_BASE ** (-2.0 * jnp.arange(halves, dtype=jnp.float32) / HEAD_SIZE)
    angles = position.astype(jnp.float32)[:, None] * inverse[None, :]
    cosine = jnp.concatenate([jnp.cos(angles), jnp.cos(angles)], axis=1)
    sine_tab = jnp.concatenate([jnp.sin(angles), jnp.sin(angles)], axis=1)
    return (cosine, sine_tab)


def rotate(field, cosine, sine_tab):
    halves = HEAD_SIZE // 2
    turned = jnp.concatenate([-field[..., halves:], field[..., :halves]], axis=-1)
    return field * cosine[:, None, :] + turned * sine_tab[:, None, :]


def attend_heads(grouped, cache_keys, cache_values, cosine, sine_tab, visible):
    score_scale = 1.0 / math.sqrt(HEAD_SIZE)
    query_rows_block = rotate(grouped[:, 0].astype(jnp.float32), cosine, sine_tab).astype(
        jnp.bfloat16
    )
    fresh_keys = rotate(grouped[:, 1].astype(jnp.float32), cosine, sine_tab).astype(jnp.bfloat16)
    gathered_keys = jnp.concatenate([cache_keys, fresh_keys], axis=0)
    gathered_values = jnp.concatenate([cache_values, grouped[:, 2]], axis=0)

    def one_head(head_parts):
        head_query, head_keys, head_values = head_parts
        logit_scores = (
            jnp.einsum("md,kd->mk", head_query, head_keys, preferred_element_type=jnp.float32)
            * score_scale
        )
        logit_scores = jnp.where(visible, logit_scores, -1e30)
        top_score = jnp.max(logit_scores, axis=1, keepdims=True)
        weight = jnp.exp(logit_scores - top_score)
        softmax_weights = (weight / jnp.sum(weight, axis=1, keepdims=True)).astype(jnp.bfloat16)
        return jnp.einsum(
            "mk,kd->md", softmax_weights, head_values, preferred_element_type=jnp.float32
        ).astype(jnp.bfloat16)

    heads_out = lax.map(
        one_head,
        (
            query_rows_block.transpose(1, 0, 2),
            gathered_keys.transpose(1, 0, 2),
            gathered_values.transpose(1, 0, 2),
        ),
    )
    return heads_out.transpose(1, 0, 2)


def on_device(
    qkv_rows,
    row_request,
    request_owner,
    cached_len,
    page_table,
    kv_pages,
    residual,
    out_weight,
    norm_gain,
):
    row_count = qkv_rows.shape[0]
    head_cols = qkv_rows.shape[2]
    heads_here = head_cols // HEAD_SIZE
    devices = lax.axis_size("req")
    slot_cap = 5 * row_count // (2 * devices)
    buffer_len = devices * slot_cap
    device_ids = jnp.arange(devices, dtype=jnp.int32)
    matches = row_request[:, None] == device_ids[None, :]
    owner_dev = jnp.sum(jnp.where(matches, request_owner[None, :], 0), axis=1)
    sends_to = (owner_dev[:, None] == device_ids[None, :]).astype(jnp.int32)
    earlier = jnp.cumsum(sends_to, axis=0) - sends_to
    slot_in = jnp.sum(earlier * sends_to, axis=1)
    target = owner_dev * slot_cap + slot_in
    counts = jnp.sum(sends_to, axis=0)
    outgoing = jnp.zeros((buffer_len, 3, head_cols), qkv_rows.dtype).at[target].set(qkv_rows)
    length = cached_len[0]
    pool_pages = kv_pages[page_table[0]]
    cache_span = pool_pages.shape[0] * pool_pages.shape[2]
    cache_keys = pool_pages[:, 0].reshape(cache_span, heads_here, HEAD_SIZE)
    cache_values = pool_pages[:, 1].reshape(cache_span, heads_here, HEAD_SIZE)
    arrived, arrived_counts = (
        lax.all_to_all(
            outgoing.reshape(devices, slot_cap, 3, head_cols),
            "req",
            split_axis=0,
            concat_axis=0,
            tiled=True,
        ),
        lax.all_to_all(counts, "req", split_axis=0, concat_axis=0, tiled=True),
    )
    live_slot = (jnp.arange(slot_cap, dtype=jnp.int32)[None, :] < arrived_counts[:, None]).reshape(
        buffer_len
    )
    live_int = live_slot.astype(jnp.int32)
    new_rank = jnp.cumsum(live_int) - live_int
    cosine, sine_tab = rope_tables(length + new_rank)
    cache_ok = jnp.broadcast_to(
        (jnp.arange(cache_span, dtype=jnp.int32) < length)[None, :], (buffer_len, cache_span)
    )
    new_ok = live_slot[None, :] & (new_rank[None, :] <= new_rank[:, None])
    visible = jnp.concatenate([cache_ok, new_ok], axis=1)
    cosine, sine_tab, visible = (cosine, sine_tab, visible)
    grouped = arrived.reshape(buffer_len, 3, heads_here, HEAD_SIZE)
    result = attend_heads(grouped, cache_keys, cache_values, cosine, sine_tab, visible)
    returned = lax.all_to_all(
        result.reshape(devices, slot_cap, head_cols), "req", split_axis=0, concat_axis=0, tiled=True
    )
    attn_rows = returned.reshape(buffer_len, head_cols)[target]
    partial_sum = jnp.dot(attn_rows, out_weight, preferred_element_type=jnp.float32)
    share_cols = residual.shape[1]
    whole_sum = lax.psum(partial_sum.astype(jnp.bfloat16), "tp").astype(jnp.float32)
    mixed_cols = lax.dynamic_slice_in_dim(
        whole_sum, lax.axis_index("tp") * share_cols, share_cols, 1
    )
    hidden = residual.astype(jnp.float32) + mixed_cols
    square_sum = lax.psum(jnp.sum(hidden * hidden, axis=1), "tp")
    inv_rms = lax.rsqrt(square_sum / D + EPS)
    normed = hidden * inv_rms[:, None] * norm_gain.astype(jnp.float32)[None, :]
    return (hidden.astype(jnp.bfloat16), normed.astype(jnp.bfloat16))


def solution(mesh):
    return jax.shard_map(
        on_device,
        mesh=mesh,
        in_specs=(
            P("req", None, "tp"),
            P("req"),
            P(),
            P("req"),
            P("req", None),
            P("req", None, None, "tp"),
            P("req", "tp"),
            P("tp", None),
            P("tp"),
        ),
        out_specs=(P("req", "tp"), P("req", "tp")),
        check_vma=False,
    )
```

profile of v0, /device:TPU:8, one launch (start us, length us, event | category | flops | bytes accessed | tf_op | source)
XLA Modules:
  0.0 280.5 jit_solution(1655667734073437765)
XLA Ops:
  7.2 1.0 select_reduce_fusion
  8.2 0.1 copy.37
  8.3 0.2 fusion.23
  8.6 0.2 fusion.22
  8.8 0.7 copy.41
  9.6 17.4 %all-to-all-start.1 = ((s32[128,1,1]{2,1,0:T(1,128)}), s32[128,1,1]{2,1,0:T(1,128)S(1)}, u32[]{:S(2)}, u32[]{:S(2)}) async-start(s32[128,1,1]{2,1,0:T(1,128)} %copy.41), calls=%async_computation.1 | async-start | bytes 131072 | tf_op jit(solution)/shard_map/all_to_all | solution.py:101
  27.0 1.6 copy.39
  28.5 1.8 broadcast_in_dim.25
  30.3 27.1 %scatter_fusion = bf16[640,3,384]{2,1,0:T(4,128)(2,1)} fusion(bf16[640,3,384]{2,1,0:T(4,128)(2,1)} %broadcast_in_dim.25, s32[256]{0:T(256)S(1)} %bitcast.92, bf16[256,3,384]{2,1,0:T(4,128)(2,1)S(1)} %copy.39), kind=kCustom, calls=%fused_computation.2 | custom fusion | bytes 1770496 | tf_op jit(solution)/shard_map/scatter | solution.py:87
  57.5 14.4 %all-to-all-start = ((bf16[128,5,3,384]{3,2,1,0:T(4,128)(2,1)}), bf16[128,5,3,384]{3,2,1,0:T(4,128)(2,1)}, u32[]{:S(2)}, u32[]{:S(2)}) async-start(bf16[128,5,3,384]{3,2,1,0:T(4,128)(2,1)} %bitcast.86), calls=%async_computation | async-start | bytes 3932160 | tf_op jit(solution)/shard_map/all_to_all | solution.py:94
  72.6 3.3 %gather_fusion = bf16[8,2,128,384]{3,2,1,0:T(8,128)(2,1)} fusion(bf16[8,2,128,384]{3,2,1,0:T(8,128)(2,1)} %param.16, s32[1024]{0:T(1024)S(1)} %pad_clamp_fusion.1), kind=kCustom, calls=%fused_computation | custom fusion | bytes 3145760 | tf_op jit(solution)/shard_map/gather | solution.py:89
  75.9 2.8 fusion.29
  78.6 1.6 copy.42
  80.3 1.2 reshape_squeeze.6
  81.5 1.6 copy.44
  83.1 1.2 reshape_squeeze.7
  84.4 2.4 reduce
  86.7 0.1 fusion.26
  86.8 0.2 lt.77
  87.0 0.2 reshape.203
  87.2 0.3 reduce-window.19
  87.5 0.1 slice.43
  87.6 0.1 slice_reduce_fusion
  87.7 0.1 add_convert_fusion
  87.8 1.2 multiply_cosine_fusion
  89.0 1.1 pad_maximum_fusion
  90.1 0.3 compare_and_fusion
  90.5 0.4 pad_add_fusion
  90.8 30.4 %all-to-all-done = bf16[128,5,3,384]{3,2,1,0:T(4,128)(2,1)} async-done(((bf16[128,5,3,384]{3,2,1,0:T(4,128)(2,1)}), bf16[128,5,3,384]{3,2,1,0:T(4,128)(2,1)}, u32[]{:S(2)}, u32[]{:S(2)}) %all-to-all-start) | async-done | bytes 1474592 | tf_op jit(solution)/shard_map/all_to_all | solution.py:94
  121.3 5.9 %reshape.198 = bf16[640,3,4,96]{3,2,1,0:T(4,128)(2,1)} reshape(bf16[128,5,3,384]{3,2,1,0:T(4,128)(2,1)} %all-to-all-done) | data formatting | bytes 2949120 | tf_op jit(solution)/shard_map/reshape | solution.py:115
  127.2 2.7 slice_bitcast_fusion
  129.9 1.5 slice_negate_fusion
  131.4 0.1 copy-done.6
  131.5 2.7 fusion.16
  134.2 0.9 copy.46
  135.1 2.1 copy.43
  137.2 2.1 copy.45
  139.4 2.5 maximum_bitcast_fusion
  141.9 1.2 maximum_bitcast_fusion.1
  143.1 22.0 %while.10 = (s32[]{:T(128)}, bf16[4,640,96]{1,2,0:T(8,128)(2,1)}, bf16[4,640,96]{2,1,0:T(8,128)(2,1)}, bf16[4,1664,96]{1,2,0:T(8,128)(2,1)}, pred[640,1664]{1,0:...) while((s32[]{:T(128)}, bf16[4,640,96]{1,2,0:T(8,128)(2,1)}, bf16[4,640,96]{2,1,0:T(8,128)(2,1)}, ...), condition=%wide.region_11.12_spmd, body=%wide.region_8.11_spmd.sunk | while | flops 417524480 | bytes 14785109 | solution.py:51
  143.1 2.1 fusion.37
  145.2 0.7 fusion.38
  145.9 2.6 fusion.39
  148.6 2.1 fusion.37
  150.7 0.7 fusion.38
  151.4 2.7 fusion.39
  154.1 2.1 fusion.37
  156.2 0.7 fusion.38
  156.9 2.6 fusion.39
  159.6 2.1 fusion.37
  161.7 0.7 fusion.38
  162.4 2.6 fusion.39
  165.1 1.7 copy.49
  166.8 1.7 reshape.200
  168.4 7.9 %all-to-all-start.2 = ((bf16[128,5,384]{2,1,0:T(8,128)(2,1)}), bf16[128,5,384]{2,1,0:T(8,128)(2,1)}, u32[]{:S(2)}, u32[]{:S(2)}) async-start(bf16[128,5,384]{2,1,0:T(8,128)(2,1)} %reshape.200), calls=%async_computation.2 | async-start | bytes 1572864 | tf_op jit(solution)/shard_map/all_to_all | solution.py:117
  176.4 25.5 %all-to-all-done.2 = bf16[128,5,384]{2,1,0:T(8,128)(2,1)} async-done(((bf16[128,5,384]{2,1,0:T(8,128)(2,1)}), bf16[128,5,384]{2,1,0:T(8,128)(2,1)}, u32[]{:S(2)}, u32[]{:S(2)}) %all-to-all-start.2) | async-done | bytes 491552 | tf_op jit(solution)/shard_map/all_to_all | solution.py:117
  201.9 1.4 reshape.201
  203.3 1.2 gather_fusion.1
  204.4 2.1 convolution_convert_fusion
  206.6 0.6 copy-done.7
  207.2 53.7 %all-reduce.2.cloned.1.call-done = bf16[256,3072]{1,0:T(8,128)(2,1)} async-done(((bf16[256,3072]{1,0:T(8,128)(2,1)}), bf16[256,3072]{1,0:T(8,128)(2,1)}) %all-reduce.2.cloned.1.call-update) | async-done | bytes 1572880 | tf_op jit(solution)/shard_map/psum | solution.py:123
  260.9 1.2 multiply_reduce_fusion
  262.1 9.5 %psum.15 = f32[256]{0:T(256)S(1)} all-reduce(f32[256]{0:T(256)S(1)} %multiply_reduce_fusion), channel_id=1, replica_groups=mesh['req'=128,'tp'=4] {'tp'}, use_global_device_ids=true, to_apply=%region_14.15 | all-reduce | flops 256 | bytes 2048 | tf_op jit(solution)/shard_map/psum | solution.py:128
  271.7 2.0 multiply_convert_fusion
  (37 shorter events, 0.3 us)
Async XLA Ops:
  7.2 197.3 %copy-start = (bf16[384,3072]{1,0:T(8,128)(2,1)S(1)}, bf16[384,3072]{1,0:T(8,128)(2,1)}, u32[]{:S(2)}) copy-start(bf16[384,3072]{1,0:T(8,128)(2,1)} %param.18) | copy-start | bytes 7077892
  9.6 47.9 %all-to-all-start.1 = ((s32[128,1,1]{2,1,0:T(1,128)}), s32[128,1,1]{2,1,0:T(1,128)S(1)}, u32[]{:S(2)}, u32[]{:S(2)}) async-start(s32[128,1,1]{2,1,0:T(1,128)} %copy.41), calls=%async_computation.1 | async-start | bytes 131072 | tf_op jit(solution)/shard_map/all_to_all | solution.py:101
  57.5 15.1 %copy-start.8 = (s32[1,8]{1,0:T(1,128)S(1)}, s32[1,8]{1,0:T(1,128)}, u32[]{:S(2)}) copy-start(s32[1,8]{1,0:T(1,128)} %param.15) | copy-start | bytes 100
  57.5 63.8 %all-to-all-start = ((bf16[128,5,3,384]{3,2,1,0:T(4,128)(2,1)}), bf16[128,5,3,384]{3,2,1,0:T(4,128)(2,1)}, u32[]{:S(2)}, u32[]{:S(2)}) async-start(bf16[128,5,3,384]{3,2,1,0:T(4,128)(2,1)} %bitcast.86), calls=%async_computation | async-start | bytes 3932160 | tf_op jit(solution)/shard_map/all_to_all | solution.py:94
  129.9 1.5 copy-start.1
  129.9 1.6 copy-start.5
  129.9 1.7 copy-start.6
  139.4 2.5 copy-start.2
  139.4 2.5 copy-start.3
  168.4 33.4 %all-to-all-start.2 = ((bf16[128,5,384]{2,1,0:T(8,128)(2,1)}), bf16[128,5,384]{2,1,0:T(8,128)(2,1)}, u32[]{:S(2)}, u32[]{:S(2)}) async-start(bf16[128,5,384]{2,1,0:T(8,128)(2,1)} %reshape.200), calls=%async_computation.2 | async-start | bytes 1572864 | tf_op jit(solution)/shard_map/all_to_all | solution.py:117
  176.3 84.6 %all-reduce.2.cloned.1.call-start = ((), (), s32[]{:S(2)}) async-start(), calls=%async_computation.3 | async-start | bytes 3145728 | tf_op jit(solution)/shard_map/psum | solution.py:123
  206.6 0.7 copy-start.7
  206.6 54.4 %copy-start.4 = (bf16[256,768]{1,0:T(8,128)(2,1)S(1)}, bf16[256,768]{1,0:T(8,128)(2,1)}, u32[]{:S(2)}) copy-start(bf16[256,768]{1,0:T(8,128)(2,1)} %param.17) | copy-start | bytes 1179652
Sparse Core Ops, SparseCore 0:
  206.7 54.1 all-reduce.1
where the time goes:
time: 282 us; the launch traced here: 281 us
  waiting for transfers between devices  110 us (39%)
  local copies, waits for them, and re-layouts  61.6 us (22%)
  starting transfers between devices  39.7 us (14%)
  other arithmetic  24 us (9%)
  matrix products  21.3 us (8%)
  between operations  14.9 us (5%)
  blocking collectives  9.53 us (3%)
    psum x1, waiting for transfers between devices, on_device(): lax.psum(partial_sum.astype(jnp.bfloat16), 'tp').astype(jnp.float32)  53.7 us
    all_to_all x1, waiting for transfers between devices, on_device(): lax.all_to_all(outgoing.reshape(devices, slot_cap, 3, head_cols), 'req',...  30.4 us
    scatter x1, local copies, waits for them, and re-layouts, on_device(): jnp.zeros((buffer_len, 3, head_cols), qkv_rows.dtype).at[target]  27.1 us
    all_to_all x1, waiting for transfers between devices, on_device(): lax.all_to_all(result.reshape(devices, slot_cap, head_cols), 'req', split...  25.5 us
    all_to_all x1, starting transfers between devices, on_device(): lax.all_to_all(counts, 'req', split_axis=0, concat_axis=0, tiled=True)  17.4 us
    all_to_all x1, starting transfers between devices, on_device(): lax.all_to_all(outgoing.reshape(devices, slot_cap, 3, head_cols), 'req',...  14.4 us
    dot_general x4, matrix products, one_head(): jnp.einsum('mk,kd->md', softmax_weights, head_values, preferred_element_t...  10.6 us
    psum x1, blocking collectives, on_device(): square_sum = lax.psum(jnp.sum(hidden * hidden, axis=1), 'tp')  9.53 us
  transfers between devices with their start and end apart: 4, of which 3 were waited for; matrix products, arithmetic and copies ran while one was open for 17% of the time, Pallas kernels for 0%

commit v1 on v0

--- a/solution.py
+++ b/solution.py
@@ -120,7 +120,9 @@
     attn_rows = returned.reshape(buffer_len, head_cols)[target]
     partial_sum = jnp.dot(attn_rows, out_weight, preferred_element_type=jnp.float32)
     share_cols = residual.shape[1]
-    whole_sum = lax.psum(partial_sum.astype(jnp.bfloat16), "tp").astype(jnp.float32)
+    whole_sum = jnp.sum(lax.all_gather(partial_sum.astype(jnp.bfloat16), "tp"), axis=0).astype(
+        jnp.float32
+    )
     mixed_cols = lax.dynamic_slice_in_dim(
         whole_sum, lax.axis_index("tp") * share_cols, share_cols, 1
     )

time: 282 us -> 297 us (1.053)
  waiting for transfers between devices: 110 us -> 119 us
  other arithmetic: 24 us -> 29.5 us
    all_gather x0 -> x1, waiting for transfers between devices: none -> 63.5 us  [on_device(): lax.all_gather(partial_sum.astype(jnp.bfloat16), 'tp')]
    psum x1 -> x0, waiting for transfers between devices: 53.7 us -> none  [on_device(): lax.psum(partial_sum.astype(jnp.bfloat16), 'tp').astype(jnp.float32)]
    reduce_sum x0 -> x1, other arithmetic: none -> 5.52 us  [on_device(): jnp.sum(lax.all_gather(partial_sum.astype(jnp.bfloat16), 'tp'), axis=0)]
  transfers between devices with their start and end apart: 4 -> 4, of which waited for: 3 -> 3; matrix products, arithmetic and copies ran while one was open for 17% -> 16% of each run, Pallas kernels for 0% -> 0%
where the time goes in v1:
time: 297 us; the launch traced here: 296 us
  waiting for transfers between devices  119 us (40%)
  local copies, waits for them, and re-layouts  61.6 us (21%)
  starting transfers between devices  39.7 us (13%)
  other arithmetic  29.5 us (10%)
  matrix products  21.3 us (7%)
  between operations  14.9 us (5%)
  blocking collectives  9.19 us (3%)
    all_gather x1, waiting for transfers between devices, on_device(): lax.all_gather(partial_sum.astype(jnp.bfloat16), 'tp')  63.5 us
    all_to_all x1, waiting for transfers between devices, on_device(): lax.all_to_all(outgoing.reshape(devices, slot_cap, 3, head_cols), 'req',...  30.4 us
    scatter x1, local copies, waits for them, and re-layouts, on_device(): jnp.zeros((buffer_len, 3, head_cols), qkv_rows.dtype).at[target]  27.1 us
    all_to_all x1, waiting for transfers between devices, on_device(): lax.all_to_all(result.reshape(devices, slot_cap, head_cols), 'req', split...  25.5 us
    all_to_all x1, starting transfers between devices, on_device(): lax.all_to_all(counts, 'req', split_axis=0, concat_axis=0, tiled=True)  17.4 us
    all_to_all x1, starting transfers between devices, on_device(): lax.all_to_all(outgoing.reshape(devices, slot_cap, 3, head_cols), 'req',...  14.4 us
    dot_general x4, matrix products, one_head(): jnp.einsum('mk,kd->md', softmax_weights, head_values, preferred_element_t...  10.6 us
    psum x1, blocking collectives, on_device(): square_sum = lax.psum(jnp.sum(hidden * hidden, axis=1), 'tp')  9.19 us
  transfers between devices with their start and end apart: 4, of which 3 were waited for; matrix products, arithmetic and copies ran while one was open for 16% of the time, Pallas kernels for 0%

profile of v1, /device:TPU:8, one launch (start us, length us, event | category | flops | bytes accessed | tf_op | source)
XLA Modules:
  0.0 295.6 jit_solution(5076373761598278166)
XLA Ops:
  7.2 1.0 select_reduce_fusion
  8.2 0.1 copy.37
  8.3 0.2 fusion.23
  8.6 0.2 fusion.22
  8.8 0.7 copy.41
  9.6 17.4 %all-to-all-start.1 = ((s32[128,1,1]{2,1,0:T(1,128)}), s32[128,1,1]{2,1,0:T(1,128)S(1)}, u32[]{:S(2)}, u32[]{:S(2)}) async-start(s32[128,1,1]{2,1,0:T(1,128)} %copy.41), calls=%async_computation.1 | async-start | bytes 131072 | tf_op jit(solution)/shard_map/all_to_all | solution.py:101
  27.0 1.6 copy.39
  28.5 1.8 broadcast_in_dim.25
  30.3 27.1 %scatter_fusion = bf16[640,3,384]{2,1,0:T(4,128)(2,1)} fusion(bf16[640,3,384]{2,1,0:T(4,128)(2,1)} %broadcast_in_dim.25, s32[256]{0:T(256)S(1)} %bitcast.94, bf16[256,3,384]{2,1,0:T(4,128)(2,1)S(1)} %copy.39), kind=kCustom, calls=%fused_computation.2 | custom fusion | bytes 1770496 | tf_op jit(solution)/shard_map/scatter | solution.py:87
  57.5 14.4 %all-to-all-start = ((bf16[128,5,3,384]{3,2,1,0:T(4,128)(2,1)}), bf16[128,5,3,384]{3,2,1,0:T(4,128)(2,1)}, u32[]{:S(2)}, u32[]{:S(2)}) async-start(bf16[128,5,3,384]{3,2,1,0:T(4,128)(2,1)} %bitcast.87), calls=%async_computation | async-start | bytes 3932160 | tf_op jit(solution)/shard_map/all_to_all | solution.py:94
  72.6 3.3 %gather_fusion = bf16[8,2,128,384]{3,2,1,0:T(8,128)(2,1)} fusion(bf16[8,2,128,384]{3,2,1,0:T(8,128)(2,1)} %param.16, s32[1024]{0:T(1024)S(1)} %pad_clamp_fusion.1), kind=kCustom, calls=%fused_computation | custom fusion | bytes 3145760 | tf_op jit(solution)/shard_map/gather | solution.py:89
  75.9 2.8 fusion.29
  78.6 1.6 copy.42
  80.3 1.2 reshape_squeeze.6
  81.5 1.6 copy.44
  83.1 1.2 reshape_squeeze.7
  84.4 2.4 reduce.1
  86.7 0.1 fusion.26
  86.8 0.2 lt.77
  87.0 0.2 reshape.203
  87.2 0.3 reduce-window.19
  87.6 0.1 slice_reduce_fusion
  87.7 0.1 add_convert_fusion
  87.8 1.2 multiply_cosine_fusion
  89.0 1.1 pad_maximum_fusion
  90.1 0.3 compare_and_fusion
  90.5 0.4 pad_add_fusion
  90.8 30.4 %all-to-all-done = bf16[128,5,3,384]{3,2,1,0:T(4,128)(2,1)} async-done(((bf16[128,5,3,384]{3,2,1,0:T(4,128)(2,1)}), bf16[128,5,3,384]{3,2,1,0:T(4,128)(2,1)}, u32[]{:S(2)}, u32[]{:S(2)}) %all-to-all-start) | async-done | bytes 1474592 | tf_op jit(solution)/shard_map/all_to_all | solution.py:94
  121.3 5.9 %reshape.198 = bf16[640,3,4,96]{3,2,1,0:T(4,128)(2,1)} reshape(bf16[128,5,3,384]{3,2,1,0:T(4,128)(2,1)} %all-to-all-done) | data formatting | bytes 2949120 | tf_op jit(solution)/shard_map/reshape | solution.py:115
  127.2 2.7 slice_bitcast_fusion
  129.9 1.5 slice_negate_fusion
  131.4 0.1 copy-done.6
  131.5 2.7 fusion.16
  134.2 0.9 copy.46
  135.1 2.1 copy.43
  137.2 2.1 copy.45
  139.4 2.5 maximum_bitcast_fusion
  141.9 1.2 maximum_bitcast_fusion.1
  143.1 22.0 %while.10 = (s32[]{:T(128)}, bf16[4,640,96]{1,2,0:T(8,128)(2,1)}, bf16[4,640,96]{2,1,0:T(8,128)(2,1)}, bf16[4,1664,96]{1,2,0:T(8,128)(2,1)}, pred[640,1664]{1,0:...) while((s32[]{:T(128)}, bf16[4,640,96]{1,2,0:T(8,128)(2,1)}, bf16[4,640,96]{2,1,0:T(8,128)(2,1)}, ...), condition=%wide.region_11.12_spmd, body=%wide.region_8.11_spmd.sunk | while | flops 417524480 | bytes 14785109 | solution.py:51
  143.1 2.1 fusion.37
  145.2 0.7 fusion.38
  145.9 2.6 fusion.39
  148.6 2.1 fusion.37
  150.7 0.7 fusion.38
  151.4 2.7 fusion.39
  154.1 2.1 fusion.37
  156.2 0.7 fusion.38
  156.9 2.6 fusion.39
  159.6 2.1 fusion.37
  161.7 0.7 fusion.38
  162.4 2.6 fusion.39
  165.1 1.7 copy.49
  166.8 1.7 reshape.200
  168.4 7.9 %all-to-all-start.2 = ((bf16[128,5,384]{2,1,0:T(8,128)(2,1)}), bf16[128,5,384]{2,1,0:T(8,128)(2,1)}, u32[]{:S(2)}, u32[]{:S(2)}) async-start(bf16[128,5,384]{2,1,0:T(8,128)(2,1)} %reshape.200), calls=%async_computation.2 | async-start | bytes 1572864 | tf_op jit(solution)/shard_map/all_to_all | solution.py:117
  176.4 25.5 %all-to-all-done.2 = bf16[128,5,384]{2,1,0:T(8,128)(2,1)} async-done(((bf16[128,5,384]{2,1,0:T(8,128)(2,1)}), bf16[128,5,384]{2,1,0:T(8,128)(2,1)}, u32[]{:S(2)}, u32[]{:S(2)}) %all-to-all-start.2) | async-done | bytes 491552 | tf_op jit(solution)/shard_map/all_to_all | solution.py:117
  201.9 1.4 reshape.201
  203.3 1.2 gather_fusion.1
  204.4 2.1 convolution_convert_fusion
  206.6 0.7 copy-done.7
  207.2 63.5 %all-gather.3.cloned.1.call-done = bf16[1024,3072]{1,0:T(8,128)(2,1)} async-done(((bf16[256,3072]{1,0:T(8,128)(2,1)}), bf16[1024,3072]{1,0:T(8,128)(2,1)}) %all-gather.3.cloned.1.call-update) | async-done | bytes 6291472 | tf_op jit(solution)/shard_map/all_gather | solution.py:123
  270.8 5.5 %reduce_sum.60 = bf16[256,3072]{1,0:T(8,128)(2,1)} reduce(bf16[4,256,3072]{2,1,0:T(8,128)(2,1)} %bitcast.88, bf16[]{:T(256)} %constant.23.clone.1), dimensions={0}, to_apply=%region_12.13 | reduce | flops 2359296 | bytes 7864322 | tf_op jit(solution)/shard_map/reduce_sum | solution.py:123
  276.3 1.2 multiply_reduce_fusion
  277.5 9.2 %psum.7 = f32[256]{0:T(256)S(1)} all-reduce(f32[256]{0:T(256)S(1)} %multiply_reduce_fusion), channel_id=1, replica_groups=mesh['req'=128,'tp'=4] {'tp'}, use_global_device_ids=true, to_apply=%region_14.15 | all-reduce | flops 256 | bytes 2048 | tf_op jit(solution)/shard_map/psum | solution.py:130
  286.7 2.0 multiply_convert_fusion
  (38 shorter events, 0.4 us)
Async XLA Ops:
  7.2 197.3 %copy-start = (bf16[384,3072]{1,0:T(8,128)(2,1)S(1)}, bf16[384,3072]{1,0:T(8,128)(2,1)}, u32[]{:S(2)}) copy-start(bf16[384,3072]{1,0:T(8,128)(2,1)} %param.18) | copy-start | bytes 7077892
  9.6 47.9 %all-to-all-start.1 = ((s32[128,1,1]{2,1,0:T(1,128)}), s32[128,1,1]{2,1,0:T(1,128)S(1)}, u32[]{:S(2)}, u32[]{:S(2)}) async-start(s32[128,1,1]{2,1,0:T(1,128)} %copy.41), calls=%async_computation.1 | async-start | bytes 131072 | tf_op jit(solution)/shard_map/all_to_all | solution.py:101
  57.5 15.1 %copy-start.8 = (s32[1,8]{1,0:T(1,128)S(1)}, s32[1,8]{1,0:T(1,128)}, u32[]{:S(2)}) copy-start(s32[1,8]{1,0:T(1,128)} %param.15) | copy-start | bytes 100
  57.5 63.8 %all-to-all-start = ((bf16[128,5,3,384]{3,2,1,0:T(4,128)(2,1)}), bf16[128,5,3,384]{3,2,1,0:T(4,128)(2,1)}, u32[]{:S(2)}, u32[]{:S(2)}) async-start(bf16[128,5,3,384]{3,2,1,0:T(4,128)(2,1)} %bitcast.87), calls=%async_computation | async-start | bytes 3932160 | tf_op jit(solution)/shard_map/all_to_all | solution.py:94
  129.9 1.5 copy-start.1
  129.9 1.6 copy-start.5
  129.9 1.7 copy-start.6
  139.4 2.5 copy-start.2
  139.4 2.5 copy-start.3
  168.4 33.4 %all-to-all-start.2 = ((bf16[128,5,384]{2,1,0:T(8,128)(2,1)}), bf16[128,5,384]{2,1,0:T(8,128)(2,1)}, u32[]{:S(2)}, u32[]{:S(2)}) async-start(bf16[128,5,384]{2,1,0:T(8,128)(2,1)} %reshape.200), calls=%async_computation.2 | async-start | bytes 1572864 | tf_op jit(solution)/shard_map/all_to_all | solution.py:117
  176.3 94.5 %all-gather.3.cloned.1.call-start = ((), (), s32[]{:S(2)}) async-start(), calls=%async_computation.3 | async-start | bytes 7864320 | tf_op jit(solution)/shard_map/all_gather | solution.py:123
  206.6 0.7 copy-start.7
  270.8 5.5 %copy-start.4 = (bf16[256,768]{1,0:T(8,128)(2,1)S(1)}, bf16[256,768]{1,0:T(8,128)(2,1)}, u32[]{:S(2)}) copy-start(bf16[256,768]{1,0:T(8,128)(2,1)} %param.17) | copy-start | bytes 1179652
Sparse Core Ops, SparseCore 0:
  206.7 64.0 all-gather.2
